TPU v7x, 512 devices: a whole 4x8x8 slice. The times are simulated.
512 devices in a mesh: row: 16 (over z_hi, x), col: 32 (over y, z_lo, core).
Axes of the slice: x: 4, y: 8, z: 8 (z_hi: 4, z_lo: 2; z = z_hi * 2 + z_lo), core: 2. Of those that a mesh axis runs over, the one named last changes fastest.
Arguments:
- slab: float32 [16384, 16384], P('row', 'col'), may hold values from -3 to 3
- u_codes: bfloat16 [2, 32, 512, 384], P(None, 'row', 'col'), may hold values from -0.8984375 to 0.8984375
- v_codes: bfloat16 [2, 32, 1024, 384], P(None, 'row', 'col'), may hold values from -0.1875 to 0.1875
- u_scale: float32 [2, 32, 384], replicated, may hold values from 0.5 to 2.5
- v_scale: float32 [2, 32, 384], replicated, may hold values from 0.5 to 2.5
- ranks: int32 [2, 32], replicated, may hold values from 64 to 384, as said below
- d_inverse: float32 [2, 2, 2, 512], replicated, may hold values from -0.6 to 2, as said below
Outputs:
- updated: float32 [16384, 16384], P('row', 'col')
Inputs may be any that keep to these rules, and one draw needn't show every extreme that they name: `ranks`: every rank is one of 64, 128, 256 and 384; every panel has a tile of rank 384. `d_inverse`: each 2 x 2 block is symmetric positive definite, its diagonal entries between 0.5 and 2, its off-diagonal entry under 0.3 times the root of their product in magnitude.
All inputs are finite; a program needn't handle non-finite values.
Results may differ from a plain program's by a relative error of at most 0.0042.
Values may be sent and summed in bfloat16 or wider, within the bound.
No kernel may reach another device: no remote copies, remote signals or barrier semaphores. Data moves between devices by JAX's collectives and lax.ppermute only.
A program may use at most 128 MiB of HBM per device.

v0:
```python
import jax
import jax.numpy as jnp
from jax import lax
from jax.sharding import PartitionSpec as P


def from_root(block, axis, owner):
    block = jnp.where(lax.axis_index(axis) == owner, block, jnp.zeros_like(block))
    return lax.psum(block, axis)


def column_weight(u_scale_k, v_scale_k, ranks_k):
    position = lax.broadcasted_iota(jnp.int32, u_scale_k.shape, 1)
    return jnp.where(position < ranks_k[:, None], u_scale_k * v_scale_k, jnp.float32(0.0))


def apply_inverse(d_block, codes):
    shape = codes.shape
    pairs = codes.reshape(shape[:-2] + (shape[-2] // 2, 2, shape[-1]))
    even = pairs[..., 0, :].astype(jnp.float32)
    odd = pairs[..., 1, :].astype(jnp.float32)
    first = d_block[0, 0][:, None] * even + d_block[0, 1][:, None] * odd
    second = d_block[1, 0][:, None] * even + d_block[1, 1][:, None] * odd
    return jnp.stack([first, second], axis=-2).reshape(shape).astype(jnp.bfloat16)


def tile_update(width, row_u, row_v, row_weight, col_scaled, col_weight, col_u):
    inner = lax.dot_general(
        row_v, col_scaled, (((0,), (0,)), ((), ())), preferred_element_type=jnp.float32
    )
    core = (row_weight[:width, None] * inner * col_weight[None, :]).astype(jnp.bfloat16)
    left = jnp.dot(row_u, core, preferred_element_type=jnp.float32).astype(jnp.bfloat16)
    return lax.dot_general(
        left, col_u, (((1,), (1,)), ((), ())), preferred_element_type=jnp.float32
    )


def panel_update(slab_rows, row_u, row_v, col_u, col_v, d_block, weight_all, first_tile, column):
    per_row = row_u.shape[0]
    rank_most = row_u.shape[-1]
    col_scaled = apply_inverse(d_block, col_v)
    row_weight = lax.dynamic_slice_in_dim(weight_all, first_tile, per_row, 0)
    col_weight = lax.dynamic_index_in_dim(weight_all, column, 0, keepdims=False)

    def one_tile(items):
        tile_u, tile_v, tile_weight = items
        return tile_update(rank_most, tile_u, tile_v, tile_weight, col_scaled, col_weight, col_u)

    update = lax.map(one_tile, (row_u, row_v, row_weight))
    return slab_rows - update.reshape(slab_rows.shape)


def deliver_columns(pick_u, pick_v, owner_row, consume, state):
    col_u, col_v = (from_root(pick_u, "row", owner_row), from_root(pick_v, "row", owner_row))
    result = consume(col_u, col_v, state)
    return result


def local(slab, u_codes, v_codes, u_scale, v_scale, ranks, d_inverse):
    per_row = lax.axis_size("col") // lax.axis_size("row")
    column = lax.axis_index("col")
    owner_row = column // per_row
    offset = column % per_row
    first_tile = lax.axis_index("row") * per_row
    panels = u_codes.shape[0]
    for k in range(panels):
        row_u, row_v = (
            lax.all_gather(u_codes[k], "col", axis=1, tiled=True),
            lax.all_gather(v_codes[k], "col", axis=1, tiled=True),
        )
        pick_u = lax.dynamic_index_in_dim(row_u, offset, 0, keepdims=False)
        pick_v = lax.dynamic_index_in_dim(row_v, offset, 0, keepdims=False)
        weight_all = column_weight(u_scale[k], v_scale[k], ranks[k])

        def consume_one(col_u, col_v, slab_now):
            return panel_update(
                slab_now, row_u, row_v, col_u, col_v, d_inverse[k], weight_all, first_tile, column
            )

        slab = deliver_columns(pick_u, pick_v, owner_row, consume_one, slab)
    return slab


def solution(mesh):
    in_specs = (
        P("row", "col"),
        P(None, "row", "col", None),
        P(None, "row", "col", None),
        P(),
        P(),
        P(),
        P(),
    )
    out_specs = P("row", "col")
    return jax.shard_map(local, mesh=mesh, in_specs=in_specs, out_specs=out_specs, check_vma=False)
```

profile of v0, /device:TPU:16, one launch (start us, length us, event | category | flops | bytes accessed | tf_op | source)
XLA Modules:
  0.0 381.7 jit_solution(7517112665492828945)
XLA Ops:
  6.5 1.5 fusion.34
  8.0 0.0 all-gather.7.cloned.1.call-update
  8.0 0.0 all-gather.9.cloned.1.call-start
  8.1 0.7 all-gather.9.cloned.1.call-update
  8.8 0.0 all-reduce.3.cloned.1.call-start
  8.8 0.8 fusion.35
  9.6 33.7 %all-gather = bf16[1,2,512,384]{3,2,1,0:T(8,128)(2,1)S(1)} all-gather(bf16[1,2,16,384]{3,2,1,0:T(8,128)(2,1)S(1)} %get-tuple-element.135), channel_id=2, replica_groups=mesh['row'=16,'col'=32] {'col'}, dimensions={2}, use_global_device_ids=true | all-gather | bytes 811008 | tf_op jit(solution)/shard_map/all_gather | solution.py:68
  43.4 0.8 select_bitcast_fusion.1
  44.2 34.9 %all-gather.2 = bf16[1,2,512,384]{3,2,1,0:T(8,128)(2,1)S(1)} all-gather(bf16[1,2,16,384]{3,2,1,0:T(8,128)(2,1)S(1)} %get-tuple-element.136), channel_id=4, replica_groups=mesh['row'=16,'col'=32] {'col'}, dimensions={2}, use_global_device_ids=true | all-gather | bytes 811008 | tf_op jit(solution)/shard_map/all_gather | solution.py:68
  79.0 0.8 select_bitcast_fusion
  79.8 0.7 all-gather.7.cloned.1.call-done
  80.5 69.1 %all-gather.9.cloned.1.call-done = bf16[1,2,1024,384]{3,2,1,0:T(8,128)(2,1)} async-done(((bf16[1,2,32,384]{3,2,1,0:T(8,128)(2,1)}), bf16[1,2,1024,384]{3,2,1,0:T(8,128)(2,1)}) %all-gather.9.cloned.1.call-update) | async-done | bytes 1572880 | tf_op jit(solution)/shard_map/all_gather | solution.py:69
  149.6 2.4 dynamic-slice_select_fusion
  152.0 2.2 reshape.104
  154.2 1.0 copy.10
  155.2 0.3 reshape.102
  155.5 0.0 copy-start.7
  155.5 0.0 copy-start.4
  155.5 0.0 copy-start.5
  155.5 0.0 copy-start.6
  155.5 1.0 copy.8
  156.5 0.0 all-reduce.3.cloned.1.call-update
  156.6 0.0 copy-done.7
  156.6 0.1 bitcast_select_fusion.1
  156.8 189.8 %all-reduce.3.cloned.1.call-done = (bf16[512,2,384]{2,0,1:T(8,128)(2,1)}, bf16[512,384]{1,0:T(8,128)(2,1)}, bf16[512,2,384]{2,0,1:T(8,128)(2,1)}, bf16[512,384]{1,0:T(8,128)(2,1)}) async-done(((bf16[512,2,384]{2,0,1:T(8,128)(2,1)}, bf16[512,384]{1,0:T(8,128)(2,1)}, bf16[512,2,384]{2,0,1:T(8,128)(2,1)}, bf16[512,384]{1,0:T(8,128)(2,1)}), (bf16[512,2,384]{2,0,1:T(8,128)(2,1)}, bf16[512,384]{1,0:T(8,128)(2,1)}, ...) | async-done | bytes 2359312 | tf_op jit(solution)/shard_map/psum | solution.py:9
  346.7 1.5 fusion.29
  348.1 0.1 pad_maximum_fusion.1
  348.2 0.8 copy.11
  349.1 1.2 convert_element_type.45
  350.2 0.3 fusion.25
  350.6 0.1 pad_maximum_fusion
  350.7 0.8 copy.9
  351.5 0.0 copy-start.3
  351.5 1.2 convert_element_type.42
  352.7 1.6 broadcast.49.clone
  354.4 6.9 %while.21 = (s32[]{:T(128)}, f32[2,512,512]{2,1,0:T(8,128)}, bf16[2,512,384]{2,1,0:T(8,128)(2,1)S(1)}, f32[2,384]{1,0:T(2,128)S(1)}, bf16[2,1024,384]{2,1,0:T(8,...) while((s32[]{:T(128)}, f32[2,512,512]{2,1,0:T(8,128)}, ...), condition=%wide.region_7.8_spmd, body=%wide.region_6.7_spmd.sunk | while | flops 654950400 | bytes 4004973 | solution.py:49
  354.4 1.7 fusion.70
  356.1 1.7 fusion.71
  357.8 1.7 fusion.70
  359.6 1.7 fusion.71
  361.3 0.2 broadcast.49.clone.1
  361.6 0.7 copy-done
  362.3 8.8 %while.20 = (s32[]{:T(128)}, f32[2,512,512]{2,1,0:T(8,128)S(1)}, bf16[2,512,384]{2,1,0:T(8,128)(2,1)S(1)}, f32[2,384]{1,0:T(2,128)S(1)}, bf16[2,1024,384]{2,1,0:...) while((s32[]{:T(128)}, f32[2,512,512]{2,1,0:T(8,128)S(1)}, ...), condition=%wide.region_3.4_spmd, body=%wide.region_2.3_spmd.sunk | while | flops 654950400 | bytes 4004973 | solution.py:49
  362.3 2.7 fusion.63
  365.0 1.7 fusion.64
  366.7 2.7 fusion.63
  369.4 1.7 fusion.64
  371.1 4.1 %bitcast_subtract_fusion = f32[1024,512]{1,0:T(8,128)} fusion(f32[2,512,512]{2,1,0:T(8,128)} %get-tuple-element.90, f32[1024,512]{1,0:T(8,128)} %param.11, f32[2,512,512]{2,1,0:T(8,128)S(1)} %get-tuple-element.89), kind=kLoop, calls=%fused_computation.26 | loop fusion | flops 1048576 | bytes 8388608 | tf_op jit(solution)/shard_map/sub | solution.py:50
  (21 shorter events, 0.2 us)
Async XLA Ops:
  6.5 74.0 %all-gather.7.cloned.1.call-start = ((), (), s32[]{:S(2)}) async-start(), calls=%async_computation | async-start | bytes 1622016 | tf_op jit(solution)/shard_map/all_gather | solution.py:69
  8.0 141.6 %all-gather.9.cloned.1.call-start = ((), (), s32[]{:S(2)}) async-start(), calls=%async_computation.1 | async-start | bytes 1622016 | tf_op jit(solution)/shard_map/all_gather | solution.py:69
  8.8 337.9 %all-reduce.3.cloned.1.call-start = ((), (), s32[]{:S(2)}) async-start(), calls=%async_computation.2 | async-start | bytes 4718592 | tf_op jit(solution)/shard_map/psum | solution.py:9
  155.5 1.1 copy-start.7
  155.5 1.1 copy-start.4
  155.5 1.1 copy-start.5
  155.5 1.3 copy-start.6
  348.1 2.1 copy-start.2
  351.5 2.9 copy-start.1
  351.5 2.8 copy-start.3
  361.3 1.0 copy-start
Sparse Core Ops, SparseCore 0:
  9.4 70.9 all-gather.6
  82.6 67.0 all-gather.8
  156.7 189.9 all-reduce.2
where the time goes:
time: 382 us
  waiting for transfers between devices  260 us (68%)
  blocking collectives  68.6 us (18%)
  matrix products  15.6 us (4%)
  local copies, waits for them, and re-layouts  13.5 us (4%)
  between operations  13.3 us (3%)
  other arithmetic  10.1 us (3%)
    psum x1, waiting for transfers between devices, from_root(): return lax.psum(block, axis)  190 us
    all_gather x2, waiting for transfers between devices, local(): lax.all_gather(v_codes[k], 'col', axis=1, tiled=True)  69.8 us
    all_gather x2, blocking collectives, local(): lax.all_gather(u_codes[k], 'col', axis=1, tiled=True)  68.6 us
    dot_general x4, matrix products, tile_update(): lax.dot_general(row_v, col_scaled, (((0,), (0,)), ((), ())), preferred_el...  8.82 us
  transfers between devices with their start and end apart: 3, of which 3 were waited for; matrix products, arithmetic and copies ran while one was open for 1% of the time, Pallas kernels for 0%

commit v1 on v0

--- a/solution.py
+++ b/solution.py
@@ -6,7 +6,7 @@
 
 def from_root(block, axis, owner):
     block = jnp.where(lax.axis_index(axis) == owner, block, jnp.zeros_like(block))
-    return lax.psum(block, axis)
+    return jnp.sum(lax.all_gather(block, axis), axis=0)
 
 
 def column_weight(u_scale_k, v_scale_k, ranks_k):

time: 382 us -> 724 us (1.90)
  the two profiles are of different devices: /device:TPU:16 before, /device:TPU:12 now
where the time goes in v1:
time: 724 us; the launch traced here: 723 us
  waiting for transfers between devices  579 us (80%)
  blocking collectives  68.8 us (10%)
  other arithmetic  33.7 us (5%)
  matrix products  13.9 us (2%)
  between operations  13.7 us (2%)
  local copies, waits for them, and re-layouts  13.3 us (2%)
    all_gather x4, waiting for transfers between devices, from_root(): return jnp.sum(lax.all_gather(block, axis), axis=0)  512 us
    all_gather x2, blocking collectives, local(): lax.all_gather(u_codes[k], 'col', axis=1, tiled=True)  68.8 us
    all_gather x2, waiting for transfers between devices, local(): lax.all_gather(v_codes[k], 'col', axis=1, tiled=True)  66.7 us
    reduce_sum x4, other arithmetic, from_root(): return jnp.sum(lax.all_gather(block, axis), axis=0)  22 us
  transfers between devices with their start and end apart: 6, of which 5 were waited for; matrix products, arithmetic and copies ran while one was open for 5% of the time, Pallas kernels for 0%

profile of v1, /device:TPU:12, one launch (start us, length us, event | category | flops | bytes accessed | tf_op | source)
XLA Modules:
  0.0 723.0 jit_solution(13058468610059113724)
XLA Ops:
  6.5 1.5 fusion.36
  8.0 0.0 all-gather.17.cloned.1.call-start
  8.1 0.7 all-gather.17.cloned.1.call-update
  8.8 0.8 fusion.37
  9.6 35.8 %all-gather = bf16[1,2,512,384]{3,2,1,0:T(8,128)(2,1)S(1)} all-gather(bf16[1,2,16,384]{3,2,1,0:T(8,128)(2,1)S(1)} %get-tuple-element.135), channel_id=2, replica_groups=mesh['row'=16,'col'=32] {'col'}, dimensions={2}, use_global_device_ids=true | all-gather | bytes 811008 | tf_op jit(solution)/shard_map/all_gather | solution.py:68
  45.5 0.8 dynamic-slice_select_fusion.3
  46.3 0.0 all-gather.25.cloned.1.call-start
  46.3 32.9 %all-gather.2 = bf16[1,2,512,384]{3,2,1,0:T(8,128)(2,1)S(1)} all-gather(bf16[1,2,16,384]{3,2,1,0:T(8,128)(2,1)S(1)} %get-tuple-element.136), channel_id=4, replica_groups=mesh['row'=16,'col'=32] {'col'}, dimensions={2}, use_global_device_ids=true | all-gather | bytes 811008 | tf_op jit(solution)/shard_map/all_gather | solution.py:68
  79.3 0.8 dynamic-slice_select_fusion.2
  80.1 0.0 all-gather.19.cloned.1.call-start
  80.2 2.1 dynamic-slice_select_fusion.1
  82.3 0.0 all-gather.23.cloned.1.call-start
  82.4 66.7 %all-gather.17.cloned.1.call-done = bf16[1,2,1024,384]{3,2,1,0:T(8,128)(2,1)} async-done(((bf16[1,2,32,384]{3,2,1,0:T(8,128)(2,1)}), bf16[1,2,1024,384]{3,2,1,0:T(8,128)(2,1)}) %all-gather.17.cloned.1.call-update) | async-done | bytes 1572880 | tf_op jit(solution)/shard_map/all_gather | solution.py:69
  149.1 2.1 dynamic-slice_select_fusion
  151.3 0.1 bitcast_select_fusion.1
  151.5 104.8 %all-gather.21.cloned.1.call-done = bf16[16,1,512,384]{3,2,1,0:T(8,128)(2,1)} async-done(((bf16[1,1,512,384]{3,2,1,0:T(8,128)(2,1)}), bf16[16,1,512,384]{3,2,1,0:T(8,128)(2,1)}) %all-gather.21.cloned.1.call-update) | async-done | bytes 6291472 | tf_op jit(solution)/shard_map/all_gather | solution.py:9
  256.3 3.8 reduce_sum.49
  260.1 100.2 %all-gather.25.cloned.1.call-done = bf16[16,1,512,384]{3,2,1,0:T(8,128)(2,1)} async-done(((bf16[1,1,512,384]{3,2,1,0:T(8,128)(2,1)}), bf16[16,1,512,384]{3,2,1,0:T(8,128)(2,1)}) %all-gather.25.cloned.1.call-update) | async-done | bytes 6291472 | tf_op jit(solution)/shard_map/all_gather | solution.py:9
  360.3 3.8 reduce_sum.51
  364.2 162.5 %all-gather.19.cloned.1.call-done = bf16[16,1,1024,384]{3,2,1,0:T(8,128)(2,1)} async-done(((bf16[1,1,1024,384]{3,2,1,0:T(8,128)(2,1)}), bf16[16,1,1024,384]{3,2,1,0:T(8,128)(2,1)}) %all-gather.19.cloned.1.call-update) | async-done | bytes 12582928 | tf_op jit(solution)/shard_map/all_gather | solution.py:9
  526.7 7.5 %reduce_sum.48 = bf16[1024,384]{1,0:T(8,128)(2,1)} reduce(bf16[16,1,1024,384]{3,2,1,0:T(8,128)(2,1)} %all-gather.19.cloned.1.call-done, bf16[]{:T(256)} %constant.85.clone.1), dimensions={0,1}, to_apply=%region_0.1 | reduce | flops 5898240 | bytes 13369346 | tf_op jit(solution)/shard_map/reduce_sum | solution.py:9
  534.2 2.2 reshape.90
  536.3 1.1 fusion.34
  537.4 0.3 fusion.25
  537.8 0.1 pad_maximum_fusion
  537.9 0.8 copy.10
  538.7 1.2 convert_element_type.50
  539.9 1.6 broadcast.45.clone.1
  541.5 7.1 while.20
  541.5 1.8 fusion.65
  543.3 1.8 fusion.66
  545.1 1.7 fusion.65
  546.8 1.7 fusion.66
  548.5 144.3 %all-gather.23.cloned.1.call-done = bf16[16,1,1024,384]{3,2,1,0:T(8,128)(2,1)} async-done(((bf16[1,1,1024,384]{3,2,1,0:T(8,128)(2,1)}), bf16[16,1,1024,384]{3,2,1,0:T(8,128)(2,1)}) %all-gather.23.cloned.1.call-update) | async-done | bytes 12582928 | tf_op jit(solution)/shard_map/all_gather | solution.py:9
  692.9 6.8 reduce_sum.50
  699.7 0.3 reshape.92
  700.0 1.1 fusion.35
  701.1 0.3 fusion.29
  701.4 0.1 pad_maximum_fusion.1
  701.5 0.8 copy.13
  702.3 0.3 convert_element_type.53
  702.6 1.6 broadcast.45.clone
  704.2 6.9 while.21
  704.3 1.7 fusion.72
  706.0 1.7 fusion.73
  707.7 1.7 fusion.72
  709.5 1.7 fusion.73
  711.2 4.9 bitcast_subtract_fusion
  (29 shorter events, 0.4 us)
Async XLA Ops:
  6.5 73.7 %all-gather.15.cloned.1.call-start = ((), (), s32[]{:S(2)}) async-start(), calls=%async_computation | async-start | bytes 1622016 | tf_op jit(solution)/shard_map/all_gather | solution.py:69
  8.0 141.1 %all-gather.17.cloned.1.call-start = ((), (), s32[]{:S(2)}) async-start(), calls=%async_computation.1 | async-start | bytes 1622016 | tf_op jit(solution)/shard_map/all_gather | solution.py:69
  8.8 247.5 %all-gather.21.cloned.1.call-start = ((), (), s32[]{:S(2)}) async-start(), calls=%async_computation.3 | async-start | bytes 6684672 | tf_op jit(solution)/shard_map/all_gather | solution.py:9
  46.3 314.0 %all-gather.25.cloned.1.call-start = ((), (), s32[]{:S(2)}) async-start(), calls=%async_computation.5 | async-start | bytes 6684672 | tf_op jit(solution)/shard_map/all_gather | solution.py:9
  80.1 71.1 %copy-start.4 = (s32[2,32]{1,0:T(2,128)S(1)}, s32[2,32]{1,0:T(2,128)}, u32[]{:S(2)}) copy-start(s32[2,32]{1,0:T(2,128)} %param.16) | copy-start | bytes 772
  80.1 71.2 %copy-start.1 = (f32[2,32,384]{2,1,0:T(8,128)S(1)}, f32[2,32,384]{2,1,0:T(8,128)}, u32[]{:S(2)}) copy-start(f32[2,32,384]{2,1,0:T(8,128)} %param.15) | copy-start | bytes 294916
  80.1 71.2 %copy-start.2 = (f32[2,32,384]{2,1,0:T(8,128)S(1)}, f32[2,32,384]{2,1,0:T(8,128)}, u32[]{:S(2)}) copy-start(f32[2,32,384]{2,1,0:T(8,128)} %param.14) | copy-start | bytes 294916
  80.1 446.5 %all-gather.19.cloned.1.call-start = ((), (), s32[]{:S(2)}) async-start(), calls=%async_computation.2 | async-start | bytes 13369344 | tf_op jit(solution)/shard_map/all_gather | solution.py:9
  82.3 69.1 %copy-start.3 = (f32[2,2,2,512]{3,2,1,0:T(2,128)S(1)}, f32[2,2,2,512]{3,2,1,0:T(2,128)}, u32[]{:S(2)}) copy-start(f32[2,2,2,512]{3,2,1,0:T(2,128)} %param.17) | copy-start | bytes 49156
  82.3 610.5 %all-gather.23.cloned.1.call-start = ((), (), s32[]{:S(2)}) async-start(), calls=%async_computation.4 | async-start | bytes 13369344 | tf_op jit(solution)/shard_map/all_gather | solution.py:9
  539.9 1.6 copy-start
Sparse Core Ops, SparseCore 0:
  9.4 70.6 all-gather.14
  82.2 66.8 all-gather.16
  152.1 104.1 all-gather.20
  259.2 101.0 all-gather.24
  363.2 163.4 all-gather.18
  529.5 163.3 all-gather.22
